TPU v7x, 512 devices: a whole 4x4x16 slice. The times are simulated.
512 devices in a mesh: group: 4 (over z_hi), shard: 16 (over z_lo, y), tensor: 8 (over x, core).
Axes of the slice: x: 4, y: 4, z: 16 (z_hi: 4, z_lo: 4; z = z_hi * 4 + z_lo), core: 2. Of those that a mesh axis runs over, the one named last changes fastest.
Arguments:
- layer_delta: bfloat16 [4, 2, 4, 224, 4864], P('group', None, None, 'shard', 'tensor'), may hold values from -6 to 6
- emb_left: bfloat16 [4, 4, 19200, 64], P('group', None, ('shard', 'tensor')), may hold values from -6 to 6
- emb_right: bfloat16 [4, 64, 896], P('group'), may hold values from -0.75 to 0.75
- layer_weight: float32 [2, 896, 4864], P(None, ('group', 'shard'), 'tensor'), may hold values from -6 to 6
- layer_momentum: float32 [2, 896, 4864], P(None, ('group', 'shard'), 'tensor'), may hold values from -4 to 4
- emb_weight: float32 [76800, 896], P(('group', 'shard', 'tensor')), may hold values from -6 to 6
- emb_momentum: float32 [76800, 896], P(('group', 'shard', 'tensor')), may hold values from -4 to 4
Outputs:
- new_layer_weight: float32 [2, 896, 4864], P(None, ('group', 'shard'), 'tensor')
- new_layer_momentum: float32 [2, 896, 4864], P(None, ('group', 'shard'), 'tensor')
- layer_blocks: bfloat16 [2, 896, 4864], P(None, None, 'tensor')
- new_emb_weight: float32 [76800, 896], P(('group', 'shard', 'tensor'))
- new_emb_momentum: float32 [76800, 896], P(('group', 'shard', 'tensor'))
All inputs are finite; a program needn't handle non-finite values.
Results may differ from a plain program's by a relative error of at most 0.0095.
Values may be sent and summed in bfloat16 or wider, within the bound.
No kernel may reach another device: no remote copies, remote signals or barrier semaphores. Data moves between devices by JAX's collectives and lax.ppermute only.
A program may use at most 64 MiB of HBM per device.

v0:
```python
import jax
import jax.numpy as jnp
from jax import lax
from jax.sharding import PartitionSpec as P

rate_outer = 0.7
beta_outer = 0.9


def on_device(
    layer_delta, emb_left, emb_right, layer_weight, layer_momentum, emb_weight, emb_momentum
):
    groups = lax.axis_size("group")
    summed = lax.psum_scatter(
        layer_delta.astype(jnp.float32).astype(jnp.bfloat16),
        "group",
        scatter_dimension=2,
        tiled=True,
    ).astype(jnp.float32)
    layer_mean = summed.reshape(layer_weight.shape) / groups
    new_layer_momentum = beta_outer * layer_momentum + layer_mean
    new_layer_weight = layer_weight - rate_outer * (layer_mean + beta_outer * new_layer_momentum)
    pieces = new_layer_weight.astype(jnp.bfloat16)
    layer_blocks = lax.all_gather(pieces, ("group", "shard"), axis=1, tiled=True)
    terms = jnp.einsum("qnr,rd->qnd", emb_left[0], emb_right[0], preferred_element_type=jnp.float32)
    total = lax.psum_scatter(
        terms.astype(jnp.bfloat16), "group", scatter_dimension=0, tiled=True
    ).astype(jnp.float32)[0]
    emb_mean = total / groups
    new_emb_momentum = beta_outer * emb_momentum + emb_mean
    new_emb_weight = emb_weight - rate_outer * (emb_mean + beta_outer * new_emb_momentum)
    return (new_layer_weight, new_layer_momentum, layer_blocks, new_emb_weight, new_emb_momentum)


def solution(mesh):
    placed = (
        P("group", None, None, "shard", "tensor"),
        P("group", None, ("shard", "tensor"), None),
        P("group", None, None),
        P(None, ("group", "shard"), "tensor"),
        P(None, ("group", "shard"), "tensor"),
        P(("group", "shard", "tensor"), None),
        P(("group", "shard", "tensor"), None),
    )
    return jax.shard_map(
        on_device,
        mesh=mesh,
        in_specs=placed,
        out_specs=(
            P(None, ("group", "shard"), "tensor"),
            P(None, ("group", "shard"), "tensor"),
            P(None, None, "tensor"),
            P(("group", "shard", "tensor"), None),
            P(("group", "shard", "tensor"), None),
        ),
        check_vma=False,
    )
```

profile of v0, /device:TPU:2, one launch (start us, length us, event | category | flops | bytes accessed | tf_op | source)
XLA Modules:
  0.0 299.9 jit_solution(9431584884943056190)
XLA Ops:
  7.2 0.0 copy-start
  7.2 0.0 copy-start.4
  7.2 0.0 copy-start.3
  7.2 0.0 copy-start.2
  7.2 0.0 copy-start.1
  7.2 0.0 all-reduce.4.cloned.1.call-start
  7.3 1.8 copy.14
  9.0 0.0 all-reduce.4.cloned.1.call-update
  9.1 0.0 reduce-scatter.5.cloned.1.call-start
  9.1 0.0 copy-done
  9.1 2.4 convolution_convert_fusion
  11.5 0.0 reduce-scatter.5.cloned.1.call-update
  11.5 0.0 all-gather.2.cloned.1.call-start
  11.6 1.3 dynamic-slice
  12.9 70.7 %all-reduce.4.cloned.1.call-done = bf16[1,2,4,14,608]{4,1,3,2,0:T(2,128)(2,1)} async-done(((bf16[1,2,4,14,608]{4,1,3,2,0:T(2,128)(2,1)}), bf16[1,2,4,14,608]{4,1,3,2,0:T(2,128)(2,1)}) %all-reduce.4.cloned.1.call-update) | async-done | bytes 136208
  83.6 0.0 copy-done.4
  83.6 0.0 copy-done.3
  83.6 2.2 fusion.6
  85.8 0.0 all-gather.2.cloned.1.call-update
  85.8 59.5 %reduce-scatter.5.cloned.1.call-done = bf16[1,150,896]{2,1,0:T(8,128)(2,1)} async-done(((bf16[4,150,896]{2,1,0:T(8,128)(2,1)}), bf16[1,150,896]{2,1,0:T(8,128)(2,1)}) %reduce-scatter.5.cloned.1.call-update) | async-done | bytes 268816
  145.4 0.0 copy-done.2
  145.4 0.0 copy-done.1
  145.4 2.1 fusion.1
  147.4 138.6 %all-gather.2.cloned.1.call-done = bf16[2,896,608]{2,0,1:T(2,128)(2,1)} async-done(((bf16[2,14,608]{2,0,1:T(2,128)(2,1)}), bf16[2,896,608]{2,0,1:T(2,128)(2,1)}) %all-gather.2.cloned.1.call-update) | async-done | bytes 2179088 | tf_op jit(solution)/shard_map/all_gather | solution.py:24
  286.1 7.3 %copy.15 = bf16[2,896,608]{1,2,0:T(8,128)(2,1)} copy(bf16[2,896,608]{2,0,1:T(2,128)(2,1)} %all-gather.2.cloned.1.call-done) | data formatting | bytes 4358144
Async XLA Ops:
  7.2 2.0 copy-start
  7.2 76.4 %copy-start.4 = (f32[2,14,608]{2,0,1:T(2,128)S(1)}, f32[2,14,608]{2,0,1:T(2,128)}, u32[]{:S(2)}) copy-start(f32[2,14,608]{2,0,1:T(2,128)} %param.11) | copy-start | bytes 204292
  7.2 76.4 %copy-start.3 = (f32[2,14,608]{2,0,1:T(2,128)S(1)}, f32[2,14,608]{2,0,1:T(2,128)}, u32[]{:S(2)}) copy-start(f32[2,14,608]{2,0,1:T(2,128)} %param.10) | copy-start | bytes 204292
  7.2 138.2 %copy-start.2 = (f32[150,896]{1,0:T(8,128)S(1)}, f32[150,896]{1,0:T(8,128)}, u32[]{:S(2)}) copy-start(f32[150,896]{1,0:T(8,128)} %param.13) | copy-start | bytes 1612804
  7.2 138.2 %copy-start.1 = (f32[150,896]{1,0:T(8,128)S(1)}, f32[150,896]{1,0:T(8,128)}, u32[]{:S(2)}) copy-start(f32[150,896]{1,0:T(8,128)} %param.12) | copy-start | bytes 1612804
  7.2 76.4 %all-reduce.4.cloned.1.call-start = ((), (), s32[]{:S(2)}) async-start(), calls=%async_computation.2 | async-start | bytes 286720
  9.1 136.3 %reduce-scatter.5.cloned.1.call-start = ((), (), s32[]{:S(2)}) async-start(), calls=%async_computation.3 | async-start | bytes 1361920
  11.5 274.5 %all-gather.2.cloned.1.call-start = ((), (), s32[]{:S(2)}) async-start(), calls=%async_computation.1 | async-start | bytes 2329600 | tf_op jit(solution)/shard_map/all_gather | solution.py:24
Sparse Core Ops, SparseCore 0:
  11.5 72.0 all-reduce.3
  87.0 58.2 reduce-scatter.4
  148.3 137.6 all-gather.1
where the time goes:
time: 300 us
  waiting for transfers between devices  269 us (90%)
  between operations  13.8 us (5%)
  local copies, waits for them, and re-layouts  10.4 us (3%)
  other arithmetic  4.27 us (1%)
    all_gather x1, waiting for transfers between devices, on_device(): lax.all_gather(pieces, ('group', 'shard'), axis=1, tiled=True)  139 us
    unnamed x5, waiting for transfers between devices  130 us
    unnamed x13, local copies, waits for them, and re-layouts  10.4 us
  transfers between devices with their start and end apart: 3, of which 3 were waited for; matrix products, arithmetic and copies ran while one was open for 3% of the time, Pallas kernels for 0%

commit v1 on v0

--- a/solution.py
+++ b/solution.py
@@ -21,7 +21,12 @@
     new_layer_momentum = beta_outer * layer_momentum + layer_mean
     new_layer_weight = layer_weight - rate_outer * (layer_mean + beta_outer * new_layer_momentum)
     pieces = new_layer_weight.astype(jnp.bfloat16)
-    layer_blocks = lax.all_gather(pieces, ("group", "shard"), axis=1, tiled=True)
+    layer_blocks = jnp.concatenate(
+        lax.all_to_all(
+            jnp.stack([pieces] * lax.axis_size(("group", "shard"))), ("group", "shard"), 0, 0
+        ),
+        axis=1,
+    )
     terms = jnp.einsum("qnr,rd->qnd", emb_left[0], emb_right[0], preferred_element_type=jnp.float32)
     total = lax.psum_scatter(
         terms.astype(jnp.bfloat16), "group", scatter_dimension=0, tiled=True

time: 300 us -> 254 us (0.85)
  waiting for transfers between devices: 269 us -> 211 us
  starting transfers between devices: 0.12 us -> 11 us
    all_gather x1 -> x0, waiting for transfers between devices: 139 us -> none  [on_device(): lax.all_gather(pieces, ('group', 'shard'), axis=1, tiled=True)]
    unnamed x5 -> x4, waiting for transfers between devices: 130 us -> 173 us
    all_to_all x0 -> x1, waiting for transfers between devices: none -> 37.4 us  [on_device(): lax.all_to_all(jnp.stack([pieces] * lax.axis_size(('group', 'shard'))), (...]
    all_to_all x0 -> x1, starting transfers between devices: none -> 10.9 us  [on_device(): lax.all_to_all(jnp.stack([pieces] * lax.axis_size(('group', 'shard'))), (...]
    unnamed x13 -> x9, local copies, waits for them, and re-layouts: 10.4 us -> 8.72 us
  transfers between devices with their start and end apart: 3 -> 3, of which waited for: 3 -> 3; matrix products, arithmetic and copies ran while one was open for 3% -> 2% of each run, Pallas kernels for 0% -> 0%
where the time goes in v1:
time: 254 us
  waiting for transfers between devices  211 us (83%)
  between operations  14.1 us (6%)
  local copies, waits for them, and re-layouts  11.3 us (4%)
  starting transfers between devices  11 us (4%)
  other arithmetic  4.46 us (2%)
    unnamed x4, waiting for transfers between devices  173 us
    all_to_all x1, waiting for transfers between devices, on_device(): lax.all_to_all(jnp.stack([pieces] * lax.axis_size(('group', 'shard'))), (...  37.4 us
    all_to_all x1, starting transfers between devices, on_device(): lax.all_to_all(jnp.stack([pieces] * lax.axis_size(('group', 'shard'))), (...  10.9 us
    unnamed x9, local copies, waits for them, and re-layouts  8.72 us
  transfers between devices with their start and end apart: 3, of which 3 were waited for; matrix products, arithmetic and copies ran while one was open for 2% of the time, Pallas kernels for 0%

profile of v1, /device:TPU:2, one launch (start us, length us, event | category | flops | bytes accessed | tf_op | source)
XLA Modules:
  0.0 253.9 jit_solution(11012726905625438166)
XLA Ops:
  7.2 0.0 copy-start
  7.2 0.0 all-reduce.4.cloned.1.call-start
  7.2 1.7 copy.16
  8.9 0.0 all-reduce.4.cloned.1.call-update
  9.0 1.3 dynamic-slice
  10.2 73.3 %all-reduce.4.cloned.1.call-done = bf16[1,2,4,14,608]{4,1,3,2,0:T(2,128)(2,1)} async-done(((bf16[1,2,4,14,608]{4,1,3,2,0:T(2,128)(2,1)}), bf16[1,2,4,14,608]{4,1,3,2,0:T(2,128)(2,1)}) %all-reduce.4.cloned.1.call-update) | async-done | bytes 136208
  83.6 2.4 fusion.6
  85.9 2.6 %stack.2 = bf16[64,2,14,608]{3,1,2,0:T(2,128)(2,1)} broadcast(bf16[2,14,608]{2,0,1:T(2,128)(2,1)S(1)} %get-tuple-element.17), dimensions={1,2,3} | broadcast | bytes 2213120 | tf_op jit(solution)/shard_map/stack | solution.py:26
  88.5 10.9 %all-to-all-start = ((bf16[64,2,14,608]{3,1,2,0:T(2,128)(2,1)}), bf16[64,2,14,608]{3,1,2,0:T(2,128)(2,1)S(1)}, u32[]{:S(2)}, u32[]{:S(2)}) async-start(bf16[64,2,14,608]{3,1,2,0:T(2,128)(2,1)} %stack.2), calls=%async_computation | async-start | bytes 4587520 | tf_op jit(solution)/shard_map/all_to_all | solution.py:25
  99.4 0.0 copy-start.1
  99.4 0.0 copy-start.2
  99.4 0.0 reduce-scatter.5.cloned.1.call-start
  99.5 0.0 copy-done
  99.5 2.5 convolution_convert_fusion
  102.0 0.0 reduce-scatter.5.cloned.1.call-update
  102.0 99.8 %reduce-scatter.5.cloned.1.call-done = bf16[1,150,896]{2,1,0:T(8,128)(2,1)} async-done(((bf16[4,150,896]{2,1,0:T(8,128)(2,1)}), bf16[1,150,896]{2,1,0:T(8,128)(2,1)}) %reduce-scatter.5.cloned.1.call-update) | async-done | bytes 268816
  201.8 0.0 copy-done.1
  201.8 0.0 copy-done.2
  201.8 2.1 fusion.1
  203.9 37.4 %all-to-all-done = bf16[64,2,14,608]{3,1,2,0:T(2,128)(2,1)S(1)} async-done(((bf16[64,2,14,608]{3,1,2,0:T(2,128)(2,1)}), bf16[64,2,14,608]{3,1,2,0:T(2,128)(2,1)S(1)}, u32[]{:S(2)}, u32[]{:S(2)}) %all-to-all-start) | async-done | bytes 2179104 | tf_op jit(solution)/shard_map/all_to_all | solution.py:25
  241.3 5.7 %copy.17 = bf16[2,896,608]{1,2,0:T(8,128)(2,1)} copy(bf16[2,896,608]{2,0,1:T(2,128)(2,1)S(1)} %bitcast.32) | data formatting | bytes 4358144
Async XLA Ops:
  7.2 92.3 %copy-start = (bf16[1,4,150,64]{2,3,1,0:T(8,128)(2,1)S(1)}, bf16[1,4,150,64]{2,3,1,0:T(8,128)(2,1)}, u32[]{:S(2)}) copy-start(bf16[1,4,150,64]{2,3,1,0:T(8,128)(2,1)} %param.8) | copy-start | bytes 230404
  7.2 76.4 %all-reduce.4.cloned.1.call-start = ((), (), s32[]{:S(2)}) async-start(), calls=%async_computation.2 | async-start | bytes 286720
  88.5 152.8 %all-to-all-start = ((bf16[64,2,14,608]{3,1,2,0:T(2,128)(2,1)}), bf16[64,2,14,608]{3,1,2,0:T(2,128)(2,1)S(1)}, u32[]{:S(2)}, u32[]{:S(2)}) async-start(bf16[64,2,14,608]{3,1,2,0:T(2,128)(2,1)} %stack.2), calls=%async_computation | async-start | bytes 4587520 | tf_op jit(solution)/shard_map/all_to_all | solution.py:25
  99.4 102.4 %copy-start.1 = (f32[150,896]{1,0:T(8,128)S(1)}, f32[150,896]{1,0:T(8,128)}, u32[]{:S(2)}) copy-start(f32[150,896]{1,0:T(8,128)} %param.12) | copy-start | bytes 1612804
  99.4 102.4 %copy-start.2 = (f32[150,896]{1,0:T(8,128)S(1)}, f32[150,896]{1,0:T(8,128)}, u32[]{:S(2)}) copy-start(f32[150,896]{1,0:T(8,128)} %param.13) | copy-start | bytes 1612804
  99.4 102.4 %reduce-scatter.5.cloned.1.call-start = ((), (), s32[]{:S(2)}) async-start(), calls=%async_computation.3 | async-start | bytes 1361920
Sparse Core Ops, SparseCore 0:
  11.5 72.0 all-reduce.3
  103.7 98.0 reduce-scatter.4
